TPU v7x, 32 devices: a whole 2x2x4 slice. The times are simulated.
32 devices in a mesh: groups: 2 (over x), seq: 16 (over z, y, core).
Axes of the slice: x: 2, y: 2, z: 4, core: 2. Of those that a mesh axis runs over, the one named last changes fastest.
Arguments:
- query: bfloat16 [4096, 1024], P(('groups', 'seq')), parts along dimension 0, as said below
- keys: bfloat16 [4096, 1024], P(('groups', 'seq')), parts along dimension 0, as said below
- values: bfloat16 [4096, 1024], P(('groups', 'seq')), parts along dimension 0, may hold values from -6 to 6
- out_weight: bfloat16 [1024, 2048], P('seq'), may hold values from -0.1875 to 0.1875
- grad_out: bfloat16 [4096, 2048], P(('groups', 'seq')), parts along dimension 0, may hold values from -6 to 6
- global_blocks: int32 [4], P('groups'), parts along dimension 0, may hold values from 0 to 15
- random_blocks: int32 [32, 3], P(('groups', 'seq')), parts along dimension 0, may hold values from 0 to 15, as said below
Outputs:
- layer_out: bfloat16 [4096, 2048], P(('groups', 'seq')), parts along dimension 0
- grad_query: bfloat16 [4096, 1024], P(('groups', 'seq')), parts along dimension 0
- grad_keys: bfloat16 [4096, 1024], P(('groups', 'seq')), parts along dimension 0
- grad_values: bfloat16 [4096, 1024], P(('groups', 'seq')), parts along dimension 0
- grad_weight: float32 [2048, 2048], P(('groups', 'seq')), parts along dimension 0
There are 2 independent parts, one for each index of `groups`. A program takes and returns all parts, laid end to end along the dimension named above; an argument that names none is the same for every part. Nothing has to cross between parts.
Inputs may be any that keep to these rules, and one draw needn't show every extreme that they name: `random_blocks`: random block r of query block b lies on the device that holds b or on a device beside it: it is at least max(b - 1, 0) * 1 and below min(b + 2, 16). `query`: entries lie between -12 and 12. `keys`: entries lie between -6 and 6.
All inputs are finite; a program needn't handle non-finite values.
Results may differ from a plain program's by a relative error of at most 0.012.
Values may be sent and summed in bfloat16 or wider, within the bound.
No kernel may reach another device: no remote copies, remote signals or barrier semaphores. Data moves between devices by JAX's collectives and lax.ppermute only.
A program may use at most 128 MiB of HBM per device.

v0:
```python
import math
import jax
import jax.numpy as jnp
from jax import lax
from jax.sharding import PartitionSpec as P

H = 8
BLK = 128
NEG_FILL = -1e30


def extended_2(shard, sides, width):
    for axis, dim in sides:
        count, length = (lax.axis_size(axis), shard.shape[dim])
        up = [(i, (i + 1) % count) for i in range(count - 1)]
        down = [(j, i) for i, j in up]
        last = lax.slice_in_dim(shard, length - width, length, axis=dim)
        initial = lax.slice_in_dim(shard, 0, width, axis=dim)
        before = lax.ppermute(last, axis, up)
        after = lax.ppermute(initial, axis, down)
        shard = jnp.concatenate([before, shard, after], axis=dim)
    return shard


def spread(shard, axis, root):
    mine = lax.axis_index(axis) == root
    return lax.psum(jnp.where(mine, shard, jnp.zeros_like(shard)), axis)


def window_and_random(random_rows, device, blocks_dev, total_blocks):
    local_ids = jnp.arange(blocks_dev, dtype=jnp.int32)
    global_ids = device * blocks_dev + local_ids
    offsets = jnp.array([-1, 0, 1], dtype=jnp.int32)
    neighbour_ids = global_ids[:, None] + offsets[None, :]
    window_index = local_ids[:, None] + blocks_dev + offsets[None, :]
    window_live = (neighbour_ids >= 0) & (neighbour_ids < total_blocks)
    random_index = random_rows - (device - 1) * blocks_dev
    ext_index = jnp.concatenate([window_index, random_index], axis=1)
    live_local = jnp.concatenate(
        [window_live, jnp.ones(random_rows.shape, dtype=jnp.bool_)], axis=1
    )
    return (ext_index, live_local)


def choose_blocks(extended, global_kv, ext_index, live_local, blocks_dev):
    feature_count = extended.shape[2]
    ext_blocks = extended.reshape(2, 3 * blocks_dev, BLK, feature_count)
    local_sel = jnp.take(ext_blocks, ext_index, axis=1)
    global_count = global_kv.shape[0]
    global_sel = jnp.swapaxes(global_kv, 0, 1)[:, None]
    chosen = jnp.concatenate([local_sel, global_sel], axis=2)
    listed = chosen.shape[2]
    chosen = chosen.reshape(2, blocks_dev, listed * BLK, H, feature_count // H)
    live = jnp.concatenate(
        [live_local, jnp.ones((blocks_dev, global_count), dtype=jnp.bool_)], axis=1
    )
    live_rows = jnp.repeat(live, BLK, axis=1)
    return (chosen[0], chosen[1], live_rows)


def attend_blocks(query_blocks, chosen_keys, chosen_values, live_rows):
    score_scale = 1.0 / math.sqrt(query_blocks.shape[-1])
    scores = (
        jnp.einsum("qihd,qjhd->qhij", query_blocks, chosen_keys, preferred_element_type=jnp.float32)
        * score_scale
    )
    scores = jnp.where(live_rows[:, None, None, :], scores, NEG_FILL)
    row_top = jnp.max(scores, axis=-1, keepdims=True)
    raised = jnp.exp(scores - row_top)
    soft_weights = raised / jnp.sum(raised, axis=-1, keepdims=True)
    rounded_weights = soft_weights.astype(jnp.bfloat16)
    mixed_out = jnp.einsum(
        "qhij,qjhd->qihd", rounded_weights, chosen_values, preferred_element_type=jnp.float32
    )
    return (soft_weights, rounded_weights, mixed_out.astype(jnp.bfloat16))


def attend_backward(
    query_blocks, chosen_keys, chosen_values, soft_weights, rounded_weights, upstream_blocks
):
    score_scale = 1.0 / math.sqrt(query_blocks.shape[-1])
    grad_chosen_values = jnp.einsum(
        "qhij,qihd->qjhd", rounded_weights, upstream_blocks, preferred_element_type=jnp.float32
    )
    grad_weights = jnp.einsum(
        "qihd,qjhd->qhij", upstream_blocks, chosen_values, preferred_element_type=jnp.float32
    )
    row_delta = jnp.sum(soft_weights * grad_weights, axis=-1, keepdims=True)
    grad_scores = (score_scale * soft_weights * (grad_weights - row_delta)).astype(jnp.bfloat16)
    grad_query_blocks = jnp.einsum(
        "qhij,qjhd->qihd", grad_scores, chosen_keys, preferred_element_type=jnp.float32
    )
    grad_chosen_keys = jnp.einsum(
        "qhij,qihd->qjhd", grad_scores, query_blocks, preferred_element_type=jnp.float32
    )
    return (grad_query_blocks, grad_chosen_keys, grad_chosen_values)


def fold_gradients(grad_chosen_keys, grad_chosen_values, ext_index, blocks_dev):
    stacked = jnp.stack([grad_chosen_keys, grad_chosen_values])
    listed_local = ext_index.shape[1]
    feature_count = stacked.shape[3] * stacked.shape[4]
    stacked = stacked.reshape(2, blocks_dev, -1, BLK * feature_count)
    local_part = stacked[:, :, :listed_local].reshape(
        2, blocks_dev * listed_local, BLK * feature_count
    )
    one_hot = (
        ext_index.reshape(-1)[:, None] == jnp.arange(3 * blocks_dev, dtype=jnp.int32)[None, :]
    ).astype(jnp.float32)
    grad_ext = jnp.einsum("sj,ksx->kjx", one_hot, local_part, precision=lax.Precision.HIGHEST)
    grad_ext = grad_ext.reshape(2, 3 * blocks_dev * BLK, feature_count)
    grad_global = jnp.sum(stacked[:, :, listed_local:], axis=1).reshape(2, -1, BLK, feature_count)
    return (grad_ext, grad_global)


def local(query, keys, values, out_weight, grad_out, global_blocks, random_blocks):
    tok_rows = query.shape[0]
    feature_count = query.shape[1]
    blocks_dev = tok_rows // BLK
    device = lax.axis_index("seq")
    total_blocks = blocks_dev * lax.axis_size("seq")
    paired = jnp.stack([keys, values])
    extended = extended_2(paired, (("seq", 1),), tok_rows)
    fetched = []
    for global_slot in range(global_blocks.shape[0]):
        block_id = global_blocks[global_slot]
        owner_index = block_id // blocks_dev
        fetched.append(spread(paired, "seq", owner_index))
    global_kv = jnp.stack(fetched)
    ext_index, live_local = window_and_random(random_blocks, device, blocks_dev, total_blocks)
    chosen_keys, chosen_values, live_rows = choose_blocks(
        extended, global_kv, ext_index, live_local, blocks_dev
    )
    query_blocks = query.reshape(blocks_dev, BLK, H, feature_count // H)
    soft_weights, rounded_weights, mixed_out = attend_blocks(
        query_blocks, chosen_keys, chosen_values, live_rows
    )
    attn_out = mixed_out.reshape(tok_rows, feature_count)
    columns = attn_out
    layer_sum = jnp.dot(
        columns,
        lax.all_gather(out_weight, "seq", axis=0, tiled=True),
        preferred_element_type=jnp.float32,
    )
    upstream_sum = lax.dot_general(
        grad_out,
        lax.all_gather(out_weight, "seq", axis=0, tiled=True),
        (((1,), (1,)), ((), ())),
        preferred_element_type=jnp.float32,
    )
    layer_out = layer_sum.astype(jnp.bfloat16)
    upstream_blocks = upstream_sum.astype(jnp.bfloat16).reshape(
        blocks_dev, BLK, H, feature_count // H
    )
    columns = attn_out
    grad_weight = lax.psum_scatter(
        lax.dot_general(
            columns, grad_out, (((0,), (0,)), ((), ())), preferred_element_type=jnp.float32
        ),
        "seq",
        scatter_dimension=0,
        tiled=True,
    )
    grad_query_blocks, grad_chosen_keys, grad_chosen_values = attend_backward(
        query_blocks, chosen_keys, chosen_values, soft_weights, rounded_weights, upstream_blocks
    )
    grad_ext, grad_global = fold_gradients(
        grad_chosen_keys, grad_chosen_values, ext_index, blocks_dev
    )
    rim_grads = jnp.concatenate(
        [grad_ext[:, :tok_rows], grad_ext[:, 2 * tok_rows :]], axis=1
    ).astype(jnp.bfloat16)
    arrived = extended_2(rim_grads, (("seq", 1),), tok_rows)
    global_total = lax.psum(grad_global, "seq")
    owned_mask = (
        global_blocks[:, None]
        == device * blocks_dev + jnp.arange(blocks_dev, dtype=jnp.int32)[None, :]
    ).astype(jnp.float32)
    owned_sum = jnp.einsum(
        "gj,kgx->kjx",
        owned_mask,
        global_total.reshape(2, owned_mask.shape[0], -1),
        precision=lax.Precision.HIGHEST,
    )
    grad_paired = grad_ext[:, tok_rows : 2 * tok_rows] + arrived[:, :tok_rows].astype(jnp.float32)
    grad_paired = grad_paired + arrived[:, 3 * tok_rows :].astype(jnp.float32)
    grad_paired = grad_paired + owned_sum.reshape(2, tok_rows, feature_count)
    grad_paired = grad_paired.astype(jnp.bfloat16)
    grad_query = grad_query_blocks.reshape(tok_rows, feature_count).astype(jnp.bfloat16)
    return (layer_out, grad_query, grad_paired[0], grad_paired[1], grad_weight)


def solution(mesh):
    placed = (
        P(("groups", "seq"), None),
        P(("groups", "seq"), None),
        P(("groups", "seq"), None),
        P("seq", None),
        P(("groups", "seq"), None),
        P("groups"),
        P(("groups", "seq"), None),
    )
    return jax.shard_map(
        local,
        mesh=mesh,
        in_specs=placed,
        out_specs=(
            P(("groups", "seq"), None),
            P(("groups", "seq"), None),
            P(("groups", "seq"), None),
            P(("groups", "seq"), None),
            P(("groups", "seq"), None),
        ),
        check_vma=False,
    )
```

profile of v0, /device:TPU:0, one launch (start us, length us, event | category | flops | bytes accessed | tf_op | source)
XLA Modules:
  0.0 429.1 jit_solution(10546698557166395422)
XLA Ops:
  10.0 2.1 select_bitcast_fusion.1
  14.2 3.8 collective-permute-start
  20.0 2.5 gather_fusion
  22.5 89.4 %all-reduce.6.cloned.1.call-done = (bf16[1,2,128,1024]{3,2,1,0:T(8,128)(2,1)}, bf16[1,2,128,1024]{3,2,1,0:T(8,128)(2,1)}) async-done(((bf16[1,2,128,1024]{3,2,1,0:T(8,128)(2,1)}, bf16[1,2,128,1024]{3,2,1,0:T(8,128)(2,1)}), (bf16[1,2,128,1024]{3,2,1,0:T(8,128)(2,1)}, bf16[1,2,128,1024]{3,2,1,0:T(8,128)(2,1)})) %all-reduce.6.cloned.1.call-update) | async-done | bytes 1048592 | tf_op jit(solution)/shard_map/psum | solution.py:27
  113.2 2.3 bitcast_select_fusion
  115.5 1.6 pad_maximum_fusion.1
  117.7 3.0 copy.52
  120.7 3.6 copy.58
  124.3 3.3 copy.34
  128.4 3.4 fusion.37
  131.8 32.2 %all-gather.2.cloned.1.call-done = bf16[1024,2048]{1,0:T(8,128)(2,1)} async-done(((bf16[64,2048]{1,0:T(8,128)(2,1)}), bf16[1024,2048]{1,0:T(8,128)(2,1)}) %all-gather.2.cloned.1.call-update) | async-done | bytes 4194320 | tf_op jit(solution)/shard_map/all_gather | solution.py:142
  164.0 3.7 convolution_convert_fusion.3
  167.9 5.0 %convolution_bitcast_fusion.1 = f32[1,1024,8,128]{1,3,2,0:T(8,128)} fusion(bf16[128,8,128]{0,2,1:T(8,128)(2,1)S(1)} %bitcast.154, f32[8,128,1024]{1,2,0:T(8,128)} %get-tuple-element.29, f32[8,128]{1,0:T(8,128)S(1)} %get-tuple-element.28), kind=kOutput, calls=%fused_computation.19 | convolution fusion | flops 270532608 | bytes 8654848 | tf_op jit(solution)/shard_map/qhij,qihd->qjhd/dot_general | solution.py:82
  172.9 3.1 multiply_reduce_fusion
  176.0 5.4 %copy.40 = f32[1,1024,8,128]{3,2,1,0:T(8,128)} copy(f32[1,1024,8,128]{1,3,2,0:T(8,128)} %convolution_bitcast_fusion.1) | data formatting | bytes 8388608 | tf_op jit(solution)/shard_map/qhij,qihd->qjhd/transpose | solution.py:82
  181.3 4.9 %stack.34 = f32[1,1,8,131072]{3,2,1,0:T(8,128)} reshape(f32[1,1024,8,128]{3,2,1,0:T(8,128)} %copy.40) | data formatting | bytes 8388608 | tf_op jit(solution)/shard_map/stack | solution.py:100
  186.2 4.2 multiply_convert_fusion
  191.7 4.4 %copy.37 = f32[1,1024,8,128]{3,2,1,0:T(8,128)} copy(f32[1,1024,8,128]{3,1,2,0:T(8,128)S(1)} %convolution_bitcast_fusion.2) | data formatting | bytes 8388608 | tf_op jit(solution)/shard_map/qhij,qihd->qjhd/transpose | solution.py:93
  196.1 4.9 %stack.33 = f32[1,1,8,131072]{3,2,1,0:T(8,128)} reshape(f32[1,1024,8,128]{3,2,1,0:T(8,128)} %copy.37) | data formatting | bytes 8388608 | tf_op jit(solution)/shard_map/stack | solution.py:100
  201.0 5.7 %fusion.10 = f32[2,131072,2]{1,2,0:T(2,128)} fusion(f32[1,1,8,131072]{3,2,0,1:T(8,128)} %bitcast.138, f32[1,1,8,131072]{3,2,0,1:T(8,128)} %bitcast.140), kind=kLoop, calls=%fused_computation.23 | loop fusion | flops 524288 | bytes 10485760 | tf_op jit(solution)/shard_map/gj,kgx->kjx/dot_general | solution.py:179
  206.7 4.0 dot_general.56
  211.0 3.6 convolution_convert_fusion.2
  214.6 4.5 %fusion.38 = f32[1024,2048]{1,0:T(8,128)} fusion(bf16[128,1024]{0,1:T(8,128)(2,1)S(1)} %bitcast.147, bf16[128,2048]{1,0:T(8,128)(2,1)S(1)} %copy-done), kind=kOutput, calls=%fused_computation.75 | convolution fusion | flops 536870912 | bytes 9175040 | tf_op jit(solution)/shard_map/dot_general | solution.py:157
  219.8 2.3 convolution_convert_fusion.1
  223.0 9.7 %convolution_bitcast_fusion = f32[2,3,131072]{2,1,0:T(4,128)} fusion(f32[1,1,8,131072]{3,2,0,1:T(8,128)} %bitcast.139, f32[1,1,8,131072]{3,2,0,1:T(8,128)} %bitcast.141, s32[6]{0:T(128)S(1)} %add_bitcast_fusion), kind=kOutput, calls=%fused_computation.2 | convolution fusion | flops 58195984 | bytes 11534360 | tf_op jit(solution)/shard_map/sj,ksx->kjx/dot_general | solution.py:110
  232.7 5.1 %reshape.362 = f32[2,384,1024]{2,1,0:T(8,128)} reshape(f32[2,3,131072]{2,1,0:T(4,128)} %convolution_bitcast_fusion) | data formatting | bytes 6291456 | tf_op jit(solution)/shard_map/reshape | solution.py:111
  237.8 2.3 convert.6
  241.5 3.3 collective-permute-start.2
  246.4 67.3 %all-reduce.4.cloned.1.call-done = f32[2,128,1024,2]{2,1,3,0:T(8,128)} async-done(((f32[2,128,1024,2]{2,1,3,0:T(8,128)}), f32[2,128,1024,2]{2,1,3,0:T(8,128)}) %all-reduce.4.cloned.1.call-update) | async-done | bytes 2097168 | tf_op jit(solution)/shard_map/psum | solution.py:174
  313.7 6.6 %fusion.13 = f32[1,2,128,1024]{3,0,2,1:T(1,128)S(1)} fusion(f32[2,128,1024,2]{2,1,3,0:T(8,128)} %all-reduce.4.cloned.1.call-done, s32[2]{0:T(128)S(1)} %copy-done.8, s32[]{:T(128)S(6)} %axis_index.8), kind=kOutput, calls=%fused_computation.28 | convolution fusion | flops 6291458 | bytes 3145740 | tf_op jit(solution)/shard_map/gj,kgx->kjx/dot_general | solution.py:179
  320.3 1.7 fusion.18
  322.8 99.8 %reduce-scatter.2.cloned.1.call-done = f32[64,2048]{1,0:T(8,128)} async-done(((f32[1024,2048]{1,0:T(8,128)}), f32[64,2048]{1,0:T(8,128)}) %reduce-scatter.2.cloned.1.call-update) | async-done | bytes 524304 | tf_op jit(solution)/shard_map/reduce_scatter | solution.py:156
  (64 shorter events, 15.4 us)
Async XLA Ops:
  7.2 156.8 %copy-start = (bf16[128,2048]{1,0:T(8,128)(2,1)S(1)}, bf16[128,2048]{1,0:T(8,128)(2,1)}, u32[]{:S(2)}) copy-start(bf16[128,2048]{1,0:T(8,128)(2,1)} %param.12) | copy-start | bytes 1572868
  7.2 10.8 %copy-start.12 = (s32[1,3,1]{1,2,0:T(1,128)S(1)}, s32[1,3,1]{1,2,0:T(1,128)}, u32[]{:S(2)}) copy-start(s32[1,3,1]{1,2,0:T(1,128)} %constant.63) | copy-start | bytes 40
  7.2 10.9 %copy-start.11 = (s32[3]{0:T(128)S(1)}, s32[3]{0:T(128)}, u32[]{:S(2)}) copy-start(s32[3]{0:T(128)} %constant.60.clone) | copy-start | bytes 40
  7.2 11.7 %copy-start.6 = (bf16[128,1024]{1,0:T(8,128)(2,1)S(1)}, bf16[128,1024]{1,0:T(8,128)(2,1)}, u32[]{:S(2)}) copy-start(bf16[128,1024]{1,0:T(8,128)(2,1)} %param.10) | copy-start | bytes 786436
  7.2 11.7 %copy-start.7 = (bf16[128,1024]{1,0:T(8,128)(2,1)S(1)}, bf16[128,1024]{1,0:T(8,128)(2,1)}, u32[]{:S(2)}) copy-start(bf16[128,1024]{1,0:T(8,128)(2,1)} %param.9) | copy-start | bytes 786436
  7.2 10.8 %copy-start.9 = (s32[1,3]{1,0:T(1,128)S(1)}, s32[1,3]{1,0:T(1,128)}, u32[]{:S(2)}) copy-start(s32[1,3]{1,0:T(1,128)} %param.14) | copy-start | bytes 40
  7.2 104.7 %all-reduce.6.cloned.1.call-start = ((), (), s32[]{:S(2)}) async-start(), calls=%async_computation.4 | async-start | bytes 2097152 | tf_op jit(solution)/shard_map/psum | solution.py:27
  12.1 151.9 %all-gather.2.cloned.1.call-start = ((), (), s32[]{:S(2)}) async-start(), calls=%async_computation.1 | async-start | bytes 4456448 | tf_op jit(solution)/shard_map/all_gather | solution.py:142
  12.8 300.8 %all-reduce.4.cloned.1.call-start = ((), (), s32[]{:S(2)}) async-start(), calls=%async_computation.2 | async-start | bytes 4194304 | tf_op jit(solution)/shard_map/psum | solution.py:174
  12.9 5.5 %collective-permute-start.1 = (bf16[2,128,1024]{2,1,0:T(8,128)(2,1)S(1)}, bf16[2,128,1024]{2,1,0:T(8,128)(2,1)S(1)}, u32[]{:S(2)}, u32[]{:S(2)}) collective-permute-start(bf16[2,128,1024]{2,1,0:T(8,128)(2,1)S(1)} %get-tuple-element.25), channel_id=1, source_target_pairs={{1,0},{2,1},{3,2},{4,3},{5,4},{6,5},{7,6},{8,7},{9,8},{10,9},{11,1... | collective-permute-start | bytes 1572872 | tf_op jit(solution)/shard_map/ppermute | solution.py:20
  14.2 4.7 %collective-permute-start = (bf16[2,128,1024]{2,1,0:T(8,128)(2,1)S(1)}, bf16[2,128,1024]{2,1,0:T(8,128)(2,1)}, u32[]{:S(2)}, u32[]{:S(2)}) collective-permute-start(bf16[2,128,1024]{2,1,0:T(8,128)(2,1)S(1)} %get-tuple-element.25), channel_id=1, source_target_pairs={{0,1},{1,2},{2,3},{3,4},{4,5},{5,6},{6,7},{7,8},{8,9},{9,10},{10,1... | collective-permute-start | bytes 1572872 | tf_op jit(solution)/shard_map/ppermute | solution.py:19
  124.3 3.3 copy-start.5
  167.9 5.0 %copy-start.3 = (f32[8,128,1024]{1,2,0:T(8,128)S(1)}, f32[8,128,1024]{1,2,0:T(8,128)}, u32[]{:S(2)}) copy-start(f32[8,128,1024]{1,2,0:T(8,128)} %get-tuple-element.29) | copy-start | bytes 12582916
  167.9 5.0 %copy-start.4 = (bf16[1024,8,128]{0,2,1:T(8,128)(2,1)S(1)}, bf16[1024,8,128]{0,2,1:T(8,128)(2,1)}, u32[]{:S(2)}) copy-start(bf16[1024,8,128]{0,2,1:T(8,128)(2,1)} %copy.52) | copy-start | bytes 6291460
  190.4 1.4 copy-start.1
  210.8 211.8 %reduce-scatter.2.cloned.1.call-start = ((), (), s32[]{:S(2)}) async-start(), calls=%async_computation.3 | async-start | bytes 8912896 | tf_op jit(solution)/shard_map/reduce_scatter | solution.py:156
  219.1 0.7 copy-start.10
  237.8 7.0 %copy-start.2 = (bf16[1024,2048]{1,0:T(8,128)(2,1)S(1)}, bf16[1024,2048]{1,0:T(8,128)(2,1)}, u32[]{:S(2)}) copy-start(bf16[1024,2048]{1,0:T(8,128)(2,1)} %all-gather.2.cloned.1.call-done) | copy-start | bytes 12582916
  240.1 73.6 %copy-start.8 = (s32[2]{0:T(128)S(1)}, s32[2]{0:T(128)}, u32[]{:S(2)}) copy-start(s32[2]{0:T(128)} %param.13) | copy-start | bytes 28
  240.2 80.0 %collective-permute-start.3 = (bf16[2,128,1024]{2,1,0:T(8,128)(2,1)S(1)}, bf16[2,128,1024]{2,1,0:T(8,128)(2,1)S(1)}, u32[]{:S(2)}, u32[]{:S(2)}) collective-permute-start(bf16[2,128,1024]{2,1,0:T(8,128)(2,1)S(1)} %get-tuple-element.20), channel_id=1, source_target_pairs={{1,0},{2,1},{3,2},{4,3},{5,4},{6,5},{7,6},{8,7},{9,8},{10,9},{11,1... | collective-permute-start | bytes 1572872 | tf_op jit(solution)/shard_map/ppermute | solution.py:20
  241.5 78.8 %collective-permute-start.2 = (bf16[2,128,1024]{2,1,0:T(8,128)(2,1)S(1)}, bf16[2,128,1024]{2,1,0:T(8,128)(2,1)S(1)}, u32[]{:S(2)}, u32[]{:S(2)}) collective-permute-start(bf16[2,128,1024]{2,1,0:T(8,128)(2,1)S(1)} %get-tuple-element.19), channel_id=1, source_target_pairs={{0,1},{1,2},{2,3},{3,4},{4,5},{5,6},{6,7},{7,8},{8,9},{9,10},{10,1... | collective-permute-start | bytes 1572872 | tf_op jit(solution)/shard_map/ppermute | solution.py:19
Sparse Core Ops, SparseCore 0:
  12.2 99.7 all-reduce.5
  114.1 49.8 all-gather.1
  210.9 102.7 all-reduce.3
  318.7 103.8 reduce-scatter.1
where the time goes:
time: 430 us; the launch traced here: 429 us
  waiting for transfers between devices  290 us (67%)
  local copies, waits for them, and re-layouts  46.4 us (11%)
  matrix products  41.4 us (10%)
  other arithmetic  26 us (6%)
  between operations  15.3 us (4%)
  starting transfers between devices  10.1 us (2%)
    reduce_scatter x1, waiting for transfers between devices, local(): lax.psum_scatter(lax.dot_general(columns, grad_out, (((0,), (0,)), ((), (...  99.8 us
    psum x1, waiting for transfers between devices, spread(): return lax.psum(jnp.where(mine, shard, jnp.zeros_like(shard)), axis)  89.4 us
    psum x1, waiting for transfers between devices, local(): global_total = lax.psum(grad_global, 'seq')  67.3 us
    all_gather x1, waiting for transfers between devices, local(): lax.all_gather(out_weight, 'seq', axis=0, tiled=True)  32.2 us
    another operation x2, local copies, waits for them, and re-layouts, fold_gradients(): stacked = jnp.stack([grad_chosen_keys, grad_chosen_values])  9.74 us
    dot_general x1, matrix products, fold_gradients(): jnp.einsum('sj,ksx->kjx', one_hot, local_part, precision=lax.Precision.HI...  9.71 us
  transfers between devices with their start and end apart: 8, of which 5 were waited for; matrix products, arithmetic and copies ran while one was open for 15% of the time, Pallas kernels for 0%

commit v1 on v0

--- a/solution.py
+++ b/solution.py
@@ -7,6 +7,18 @@
 H = 8
 BLK = 128
 NEG_FILL = -1e30
+
+
+def collect(x, axis, dim):
+    ways, here, step = (lax.axis_size(axis), lax.axis_index(axis), x.shape[dim])
+    line, have = (x, 1)
+    while have < ways:
+        line = jnp.concatenate(
+            [line, lax.ppermute(line, axis, [(d, (d - have) % ways) for d in range(ways)])],
+            axis=dim,
+        )
+        have = 2 * have
+    return jnp.roll(line, here * step, axis=dim)
 
 
 def extended_2(shard, sides, width):
@@ -137,11 +149,7 @@
     )
     attn_out = mixed_out.reshape(tok_rows, feature_count)
     columns = attn_out
-    layer_sum = jnp.dot(
-        columns,
-        lax.all_gather(out_weight, "seq", axis=0, tiled=True),
-        preferred_element_type=jnp.float32,
-    )
+    layer_sum = jnp.dot(columns, collect(out_weight, "seq", 0), preferred_element_type=jnp.float32)
     upstream_sum = lax.dot_general(
         grad_out,
         lax.all_gather(out_weight, "seq", axis=0, tiled=True),

time: 430 us -> 525 us (1.22)
  waiting for transfers between devices: 290 us -> 368 us
  local copies, waits for them, and re-layouts: 46.4 us -> 59.7 us
  matrix products: 41.4 us -> 36 us
    ppermute x0 -> x4, waiting for transfers between devices: none -> 141 us  [collect(): lax.ppermute(line, axis, [(d, (d - have) % ways) for d in range(ways)])]
    psum x1, waiting for transfers between devices: 67.3 us -> 7.39 us  [local(): global_total = lax.psum(grad_global, 'seq')]
    unnamed x29 -> x48, local copies, waits for them, and re-layouts: 6.39 us -> 15.6 us
    ppermute x0 -> x4, starting transfers between devices: none -> 6.64 us  [collect(): lax.ppermute(line, axis, [(d, (d - have) % ways) for d in range(ways)])]
  transfers between devices with their start and end apart: 8 -> 12, of which waited for: 5 -> 8; matrix products, arithmetic and copies ran while one was open for 15% -> 14% of each run, Pallas kernels for 0% -> 0%
where the time goes in v1:
time: 525 us; the launch traced here: 524 us
  waiting for transfers between devices  368 us (70%)
  local copies, waits for them, and re-layouts  59.7 us (11%)
  matrix products  36 us (7%)
  other arithmetic  30.4 us (6%)
  between operations  15.4 us (3%)
  starting transfers between devices  14 us (3%)
    ppermute x4, waiting for transfers between devices, collect(): lax.ppermute(line, axis, [(d, (d - have) % ways) for d in range(ways)])  141 us
    reduce_scatter x1, waiting for transfers between devices, local(): lax.psum_scatter(lax.dot_general(columns, grad_out, (((0,), (0,)), ((), (...  101 us
    psum x1, waiting for transfers between devices, spread(): return lax.psum(jnp.where(mine, shard, jnp.zeros_like(shard)), axis)  88.4 us
    all_gather x1, waiting for transfers between devices, local(): lax.all_gather(out_weight, 'seq', axis=0, tiled=True)  29.8 us
    unnamed x48, local copies, waits for them, and re-layouts  15.6 us
  transfers between devices with their start and end apart: 12, of which 8 were waited for; matrix products, arithmetic and copies ran while one was open for 14% of the time, Pallas kernels for 0%

profile of v1, /device:TPU:0, one launch (start us, length us, event | category | flops | bytes accessed | tf_op | source)
XLA Modules:
  0.0 523.8 jit_solution(12936342039565399457)
XLA Ops:
  14.1 3.1 collective-permute-start
  21.3 2.5 gather_fusion
  23.8 88.4 %all-reduce.6.cloned.1.call-done = (bf16[1,2,128,1024]{3,2,1,0:T(8,128)(2,1)}, bf16[1,2,128,1024]{3,2,1,0:T(8,128)(2,1)}) async-done(((bf16[1,2,128,1024]{3,2,1,0:T(8,128)(2,1)}, bf16[1,2,128,1024]{3,2,1,0:T(8,128)(2,1)}), (bf16[1,2,128,1024]{3,2,1,0:T(8,128)(2,1)}, bf16[1,2,128,1024]{3,2,1,0:T(8,128)(2,1)})) %all-reduce.6.cloned.1.call-update) | async-done | bytes 1048592 | tf_op jit(solution)/shard_map/psum | solution.py:39
  113.5 2.3 bitcast_select_fusion
  119.3 3.3 copy.34
  122.5 3.6 copy.57
  126.1 4.2 copy.52
  131.1 3.4 fusion.43
  134.5 29.8 %all-gather.2.cloned.1.call-done = bf16[1024,2048]{1,0:T(8,128)(2,1)} async-done(((bf16[64,2048]{1,0:T(8,128)(2,1)}), bf16[1024,2048]{1,0:T(8,128)(2,1)}) %all-gather.2.cloned.1.call-update) | async-done | bytes 4194320 | tf_op jit(solution)/shard_map/all_gather | solution.py:155
  164.3 3.7 convolution_convert_fusion.2
  168.2 5.1 convolution_bitcast_fusion.1
  173.2 3.1 multiply_reduce_fusion
  176.3 5.4 %copy.40 = f32[1,1024,8,128]{3,2,1,0:T(8,128)} copy(f32[1,1024,8,128]{1,3,2,0:T(8,128)} %convolution_bitcast_fusion.1) | data formatting | bytes 8388608 | tf_op jit(solution)/shard_map/qhij,qihd->qjhd/transpose | solution.py:94
  181.7 4.9 stack.34
  186.6 4.2 multiply_convert_fusion
  192.8 4.5 copy.37
  197.3 4.9 stack.33
  202.2 5.7 %fusion.15 = f32[2,131072,2]{1,2,0:T(2,128)} fusion(f32[1,1,8,131072]{3,2,0,1:T(8,128)} %bitcast.137, f32[1,1,8,131072]{3,2,0,1:T(8,128)} %bitcast.139), kind=kLoop, calls=%fused_computation.25 | loop fusion | flops 524288 | bytes 10485760 | tf_op jit(solution)/shard_map/gj,kgx->kjx/dot_general | solution.py:187
  207.9 4.0 dot_general.56
  212.0 3.5 convolution_convert_fusion.1
  216.2 4.5 fusion.44
  223.4 7.2 %collective-permute-done.2 = bf16[64,2048]{1,0:T(8,128)(2,1)S(1)} collective-permute-done((bf16[64,2048]{1,0:T(8,128)(2,1)S(1)}, bf16[64,2048]{1,0:T(8,128)(2,1)S(1)}, u32[]{:S(2)}, u32[]{:S(2)}) %collective-permute-start.2) | collective-permute-done | bytes 262176 | tf_op jit(solution)/shard_map/ppermute | solution.py:17
  230.7 15.5 %collective-permute-done.3 = bf16[128,2048]{1,0:T(8,128)(2,1)S(1)} collective-permute-done((bf16[128,2048]{1,0:T(8,128)(2,1)S(1)}, bf16[128,2048]{1,0:T(8,128)(2,1)S(1)}, u32[]{:S(2)}, u32[]{:S(2)}) %collective-permute-start.3) | collective-permute-done | bytes 524320 | tf_op jit(solution)/shard_map/ppermute | solution.py:17
  248.0 26.7 %collective-permute-done.4 = bf16[256,2048]{1,0:T(8,128)(2,1)S(1)} collective-permute-done((bf16[256,2048]{1,0:T(8,128)(2,1)S(1)}, bf16[256,2048]{1,0:T(8,128)(2,1)S(1)}, u32[]{:S(2)}, u32[]{:S(2)}) %collective-permute-start.4) | collective-permute-done | bytes 1048608 | tf_op jit(solution)/shard_map/ppermute | solution.py:17
  277.2 3.1 collective-permute-start.5
  282.9 91.5 %collective-permute-done.5 = bf16[512,2048]{1,0:T(8,128)(2,1)} collective-permute-done((bf16[512,2048]{1,0:T(8,128)(2,1)}, bf16[512,2048]{1,0:T(8,128)(2,1)}, u32[]{:S(2)}, u32[]{:S(2)}) %collective-permute-start.5) | collective-permute-done | bytes 2097184 | tf_op jit(solution)/shard_map/ppermute | solution.py:17
  380.8 5.7 %convolution_bitcast_fusion = f32[2,3,131072]{2,1,0:T(4,128)} fusion(f32[1,1,8,131072]{3,2,0,1:T(8,128)S(1)} %bitcast.138, f32[1,1,8,131072]{3,2,0,1:T(8,128)S(1)} %bitcast.140, s32[6]{0:T(128)S(1)} %add_bitcast_fusion), kind=kOutput, calls=%fused_computation.2 | convolution fusion | flops 58195984 | bytes 11534360 | tf_op jit(solution)/shard_map/sj,ksx->kjx/dot_general | solution.py:122
  386.5 5.1 reshape.362
  391.7 2.3 convert.6
  399.6 7.4 %all-reduce.4.cloned.1.call-done = f32[2,128,1024,2]{2,1,3,0:T(8,128)} async-done(((f32[2,128,1024,2]{2,1,3,0:T(8,128)}), f32[2,128,1024,2]{2,1,3,0:T(8,128)}) %all-reduce.4.cloned.1.call-update) | async-done | bytes 2097168 | tf_op jit(solution)/shard_map/psum | solution.py:182
  407.0 6.6 %fusion.18 = f32[1,2,128,1024]{3,0,2,1:T(1,128)S(1)} fusion(f32[2,128,1024,2]{2,1,3,0:T(8,128)} %all-reduce.4.cloned.1.call-done, s32[2]{0:T(128)S(1)} %copy-done.15, s32[]{:T(128)S(6)} %axis_index.8), kind=kOutput, calls=%fused_computation.31 | convolution fusion | flops 6291458 | bytes 3145740 | tf_op jit(solution)/shard_map/gj,kgx->kjx/dot_general | solution.py:187
  416.2 101.0 %reduce-scatter.2.cloned.1.call-done = f32[64,2048]{1,0:T(8,128)} async-done(((f32[1024,2048]{1,0:T(8,128)}), f32[64,2048]{1,0:T(8,128)}) %reduce-scatter.2.cloned.1.call-update) | async-done | bytes 524304 | tf_op jit(solution)/shard_map/reduce_scatter | solution.py:164
  (95 shorter events, 42.3 us)
Async XLA Ops:
  7.2 157.1 %copy-start = (bf16[128,2048]{1,0:T(8,128)(2,1)S(1)}, bf16[128,2048]{1,0:T(8,128)(2,1)}, u32[]{:S(2)}) copy-start(bf16[128,2048]{1,0:T(8,128)(2,1)} %param.12) | copy-start | bytes 1572868
  7.2 105.0 %all-reduce.6.cloned.1.call-start = ((), (), s32[]{:S(2)}) async-start(), calls=%async_computation.4 | async-start | bytes 2097152 | tf_op jit(solution)/shard_map/psum | solution.py:39
  12.0 152.3 %all-gather.2.cloned.1.call-start = ((), (), s32[]{:S(2)}) async-start(), calls=%async_computation.1 | async-start | bytes 4456448 | tf_op jit(solution)/shard_map/all_gather | solution.py:155
  12.7 394.2 %all-reduce.4.cloned.1.call-start = ((), (), s32[]{:S(2)}) async-start(), calls=%async_computation.2 | async-start | bytes 4194304 | tf_op jit(solution)/shard_map/psum | solution.py:182
  12.8 7.3 %collective-permute-start.1 = (bf16[2,128,1024]{2,1,0:T(8,128)(2,1)S(1)}, bf16[2,128,1024]{2,1,0:T(8,128)(2,1)S(1)}, u32[]{:S(2)}, u32[]{:S(2)}) collective-permute-start(bf16[2,128,1024]{2,1,0:T(8,128)(2,1)S(1)} %get-tuple-element.25), channel_id=1, source_target_pairs={{1,0},{2,1},{3,2},{4,3},{5,4},{6,5},{7,6},{8,7},{9,8},{10,9},{11,1... | collective-permute-start | bytes 1572872 | tf_op jit(solution)/shard_map/ppermute | solution.py:32
  14.1 6.0 %collective-permute-start = (bf16[2,128,1024]{2,1,0:T(8,128)(2,1)S(1)}, bf16[2,128,1024]{2,1,0:T(8,128)(2,1)S(1)}, u32[]{:S(2)}, u32[]{:S(2)}) collective-permute-start(bf16[2,128,1024]{2,1,0:T(8,128)(2,1)S(1)} %get-tuple-element.25), channel_id=1, source_target_pairs={{0,1},{1,2},{2,3},{3,4},{4,5},{5,6},{6,7},{7,8},{8,9},{9,10},{10,1... | collective-permute-start | bytes 1572872 | tf_op jit(solution)/shard_map/ppermute | solution.py:31
  122.5 7.8 %copy-start.14 = (bf16[128,1024]{1,0:T(8,128)(2,1)S(1)}, bf16[128,1024]{1,0:T(8,128)(2,1)}, u32[]{:S(2)}) copy-start(bf16[128,1024]{1,0:T(8,128)(2,1)} %param.8) | copy-start | bytes 786436
  168.2 5.1 copy-start.10
  168.2 5.1 copy-start.11
  190.8 1.3 copy-start.3
  211.9 305.3 %reduce-scatter.2.cloned.1.call-start = ((), (), s32[]{:S(2)}) async-start(), calls=%async_computation.3 | async-start | bytes 8912896 | tf_op jit(solution)/shard_map/reduce_scatter | solution.py:164
  215.5 0.7 copy-start.12
  220.7 1.0 copy-start.7
  221.7 58.6 %copy-start.16 = (s32[1,3]{1,0:T(1,128)S(1)}, s32[1,3]{1,0:T(1,128)}, u32[]{:S(2)}) copy-start(s32[1,3]{1,0:T(1,128)} %param.14) | copy-start | bytes 40
  221.7 58.6 %copy-start.17 = (s32[1,3]{1,0:T(1,128)S(1)}, s32[1,3]{1,0:T(1,128)}, u32[]{:S(2)}) copy-start(s32[1,3]{1,0:T(1,128)} %constant.87) | copy-start | bytes 40
  221.7 8.9 %collective-permute-start.2 = (bf16[64,2048]{1,0:T(8,128)(2,1)S(1)}, bf16[64,2048]{1,0:T(8,128)(2,1)S(1)}, u32[]{:S(2)}, u32[]{:S(2)}) collective-permute-start(bf16[64,2048]{1,0:T(8,128)(2,1)S(1)} %copy-done.7), channel_id=1, source_target_pairs={{0,15},{1,0},{2,1},{3,2},{4,3},{5,4},{6,5},{7,6},{8,7},{9,8},{10,9... | collective-permute-start | bytes 786440 | tf_op jit(solution)/shard_map/ppermute | solution.py:17
  230.6 46.6 %copy-start.8 = (bf16[64,2048]{1,0:T(8,128)(2,1)}, bf16[64,2048]{1,0:T(8,128)(2,1)S(1)}, u32[]{:S(2)}) copy-start(bf16[64,2048]{1,0:T(8,128)(2,1)S(1)} %collective-permute-done.2) | copy-start | bytes 786436
  230.6 15.5 %collective-permute-start.3 = (bf16[128,2048]{1,0:T(8,128)(2,1)S(1)}, bf16[128,2048]{1,0:T(8,128)(2,1)S(1)}, u32[]{:S(2)}, u32[]{:S(2)}) collective-permute-start(bf16[128,2048]{1,0:T(8,128)(2,1)S(1)} %pad_maximum_fusion.6), channel_id=1, source_target_pairs={{0,14},{1,15},{2,0},{3,1},{4,2},{5,3},{6,4},{7,5},{8,6},{9,7},{10,... | collective-permute-start | bytes 1572872 | tf_op jit(solution)/shard_map/ppermute | solution.py:17
  246.2 28.5 %collective-permute-start.4 = (bf16[256,2048]{1,0:T(8,128)(2,1)S(1)}, bf16[256,2048]{1,0:T(8,128)(2,1)S(1)}, u32[]{:S(2)}, u32[]{:S(2)}) collective-permute-start(bf16[256,2048]{1,0:T(8,128)(2,1)S(1)} %pad_maximum_fusion.4), channel_id=1, source_target_pairs={{0,12},{1,13},{2,14},{3,15},{4,0},{5,1},{6,2},{7,3},{8,4},{9,5},{1... | collective-permute-start | bytes 3145736 | tf_op jit(solution)/shard_map/ppermute | solution.py:17
  274.7 1.0 copy-start.5
  277.2 97.3 %collective-permute-start.5 = (bf16[512,2048]{1,0:T(8,128)(2,1)}, bf16[512,2048]{1,0:T(8,128)(2,1)}, u32[]{:S(2)}, u32[]{:S(2)}) collective-permute-start(bf16[512,2048]{1,0:T(8,128)(2,1)} %pad_maximum_fusion.2), channel_id=1, source_target_pairs={{0,8},{1,9},{2,10},{3,11},{4,12},{5,13},{6,14},{7,15},{8,0},{9,1},... | collective-permute-start | bytes 6291464 | tf_op jit(solution)/shard_map/ppermute | solution.py:17
  280.4 95.9 %copy-start.9 = (bf16[64,2048]{1,0:T(8,128)(2,1)S(1)}, bf16[64,2048]{1,0:T(8,128)(2,1)}, u32[]{:S(2)}) copy-start(bf16[64,2048]{1,0:T(8,128)(2,1)} %copy-done.8) | copy-start | bytes 786436
  281.5 94.9 %copy-start.6 = (bf16[256,2048]{1,0:T(8,128)(2,1)S(1)}, bf16[256,2048]{1,0:T(8,128)(2,1)}, u32[]{:S(2)}) copy-start(bf16[256,2048]{1,0:T(8,128)(2,1)} %copy-done.5) | copy-start | bytes 3145732
  376.3 2.2 copy-start.13
  376.5 3.6 copy-start.1
  376.5 4.3 copy-start.2
  391.7 6.3 %copy-start.4 = (bf16[8,128,1024]{1,2,0:T(8,128)(2,1)S(1)}, bf16[8,128,1024]{1,2,0:T(8,128)(2,1)}, u32[]{:S(2)}) copy-start(bf16[8,128,1024]{1,2,0:T(8,128)(2,1)} %copy-done.3) | copy-start | bytes 6291460
  394.0 13.0 %copy-start.15 = (s32[2]{0:T(128)S(1)}, s32[2]{0:T(128)}, u32[]{:S(2)}) copy-start(s32[2]{0:T(128)} %param.13) | copy-start | bytes 28
  395.1 18.4 %collective-permute-start.6 = (bf16[2,128,1024]{2,1,0:T(8,128)(2,1)}, bf16[2,128,1024]{2,1,0:T(8,128)(2,1)S(1)}, u32[]{:S(2)}, u32[]{:S(2)}) collective-permute-start(bf16[2,128,1024]{2,1,0:T(8,128)(2,1)} %get-tuple-element.19), channel_id=1, source_target_pairs={{0,1},{1,2},{2,3},{3,4},{4,5},{5,6},{6,7},{7,8},{8,9},{9,10},{10,1... | collective-permute-start | bytes 1572872 | tf_op jit(solution)/shard_map/ppermute | solution.py:31
  396.7 16.9 %collective-permute-start.7 = (bf16[2,128,1024]{2,1,0:T(8,128)(2,1)}, bf16[2,128,1024]{2,1,0:T(8,128)(2,1)}, u32[]{:S(2)}, u32[]{:S(2)}) collective-permute-start(bf16[2,128,1024]{2,1,0:T(8,128)(2,1)} %get-tuple-element.20), channel_id=1, source_target_pairs={{1,0},{2,1},{3,2},{4,3},{5,4},{6,5},{7,6},{8,7},{9,8},{10,9},{11,1... | collective-permute-start | bytes 1572872 | tf_op jit(solution)/shard_map/ppermute | solution.py:32
Sparse Core Ops, SparseCore 0:
  12.1 100.0 all-reduce.5
  114.4 49.8 all-gather.1
  212.0 194.8 all-reduce.3
  412.0 105.1 reduce-scatter.1
